TPU v7x, 32 devices: a whole 2x2x4 slice. The times are simulated.
32 devices in a mesh: dp: 8 (over y, x, core), space: 4 (over z).
Axes of the slice: x: 2, y: 2, z: 4, core: 2. Of those that a mesh axis runs over, the one named last changes fastest.
Arguments:
- volume: bfloat16 [8, 32, 8, 16, 128], P('dp', None, 'space')
- out_grad: bfloat16 [8, 32, 8, 16, 128], P('dp', None, 'space'), may hold values from -0.016479492 to 0.016479492
- kernel: bfloat16 [32, 864], replicated, may hold values from -0.21875 to 0.21875
- sample_idx: int32 [8, 4096], P('dp', 'space'), may hold values from 0 to 4095
- a_inverse: float32 [864, 864], P('space')
- g_inverse: float32 [32, 32], replicated
Outputs:
- conv_out: bfloat16 [8, 32, 8, 16, 128], P('dp', None, 'space')
- a_factor: float32 [864, 864], P('dp', 'space')
- g_factor: float32 [32, 32], replicated
- pre_grad: float32 [32, 864], replicated
Inputs may be any that keep to these rules, and one draw needn't show every extreme that they name: `sample_idx`: column s of a sample's row names a cell of slab s // 1024, as the number z * 16 * 128 + y * 128 + x counted within that slab of 2 planes.
All inputs are finite; a program needn't handle non-finite values.
Results may differ from a plain program's by a relative error of at most 0.0085.
Values may be sent and summed in bfloat16 or wider, within the bound.
No kernel may reach another device: no remote copies, remote signals or barrier semaphores. Data moves between devices by JAX's collectives and lax.ppermute only.
A program may use at most 128 MiB of HBM per device.

v0:
```python
import jax
import jax.numpy as jnp
from jax import lax
from jax.sharding import PartitionSpec as P


def padded_2(cells, sides, width):
    for axis, dim in sides:
        count = lax.axis_size(axis)
        ends = count - 1
        head = lax.slice_in_dim(cells, 0, width, axis=dim)
        tail = lax.slice_in_dim(cells, cells.shape[dim] - width, cells.shape[dim], axis=dim)
        cells = jnp.concatenate(
            [
                lax.ppermute(tail, axis, [(i, (i + 1) % count) for i in range(ends)]),
                cells,
                lax.ppermute(head, axis, [((i + 1) % count, i) for i in range(ends)]),
            ],
            axis=dim,
        )
    return cells


def on_device(volume, out_grad, kernel, sample_idx, a_inverse, g_inverse):
    highest = lax.Precision.HIGHEST
    f32 = jnp.float32
    channels = volume.shape[1]
    planes = volume.shape[2]
    y_cells = volume.shape[3]
    x_cells = volume.shape[4]
    cells = planes * y_cells * x_cells
    patch = kernel.shape[1]
    n_dp = lax.axis_size("dp")
    n_sp = lax.axis_size("space")
    contract_cells = (((1,), (1,)), ((), ()))
    block = padded_2(volume, (("space", 2),), 1)
    padded = jnp.pad(block[0], ((0, 0), (0, 0), (1, 1), (1, 1)))
    taps = [
        padded[:, dz : dz + planes, dy : dy + y_cells, dx : dx + x_cells]
        for dz in range(3)
        for dy in range(3)
        for dx in range(3)
    ]
    patches_t = jnp.stack(taps, axis=1).reshape(patch, cells)
    grad_flat = out_grad[0].reshape(channels, cells)
    forward = jnp.dot(kernel, patches_t, preferred_element_type=f32)
    conv_out = forward.astype(jnp.bfloat16).reshape(1, channels, planes, y_cells, x_cells)
    grad_w = lax.dot_general(grad_flat, patches_t, contract_cells, preferred_element_type=f32)
    g_part = lax.dot_general(grad_flat, grad_flat, contract_cells, preferred_element_type=f32)
    cell_ids = sample_idx[0]
    counts = jnp.sum(
        (cell_ids[:, None] == jnp.arange(cells, dtype=jnp.int32)[None, :]).astype(f32), axis=0
    )
    weighted = patches_t.astype(f32) * counts[None, :]
    high = weighted.astype(jnp.bfloat16)
    low = (weighted - high.astype(f32)).astype(jnp.bfloat16)
    total_samples = sample_idx.shape[1] * n_sp * n_dp
    a_part = (
        lax.dot_general(high, patches_t, contract_cells, preferred_element_type=f32)
        + lax.dot_general(low, patches_t, contract_cells, preferred_element_type=f32)
    ) / jnp.float32(total_samples)
    rows = patch // n_dp
    cols = patch // n_sp
    a_blocks = (
        a_part.astype(jnp.bfloat16)
        .reshape(n_dp, rows, n_sp, cols)
        .transpose(0, 2, 1, 3)
        .reshape(n_dp * n_sp, rows, cols)
    )
    a_factor = lax.psum_scatter(a_blocks, ("dp", "space"), scatter_dimension=0, tiled=True)
    a_factor = a_factor.reshape(rows, cols).astype(f32)
    both = lax.psum(jnp.concatenate([grad_w, g_part], axis=1), ("dp", "space"))
    grad_sum = both[:, :patch]
    g_factor = both[:, patch:]
    left = jnp.dot(g_inverse, grad_sum, precision=highest)
    own_rows = a_inverse.shape[0]
    left_rows = lax.dynamic_slice_in_dim(left, lax.axis_index("space") * own_rows, own_rows, axis=1)
    pre_grad = lax.psum(jnp.dot(left_rows, a_inverse, precision=highest), "space")
    return (conv_out, a_factor, g_factor, pre_grad)


def solution(mesh):
    placed = (
        P("dp", None, "space", None, None),
        P("dp", None, "space", None, None),
        P(),
        P("dp", "space"),
        P("space", None),
        P(),
    )
    return jax.shard_map(
        on_device,
        mesh=mesh,
        in_specs=placed,
        out_specs=(P("dp", None, "space", None, None), P("dp", "space"), P(), P()),
        check_vma=False,
    )
```

profile of v0, /device:TPU:0, one launch (start us, length us, event | category | flops | bytes accessed | tf_op | source)
XLA Modules:
  0.0 373.9 jit_solution(7109457592317233880)
XLA Ops:
  7.2 1.1 fusion.59
  8.3 4.9 %collective-permute-start = (bf16[1,32,1,16,128]{4,3,2,1,0:T(8,128)(2,1)S(1)}, bf16[1,32,1,16,128]{4,3,2,1,0:T(8,128)(2,1)S(1)}, u32[]{:S(2)}, u32[]{:S(2)}) collective-permute-start(bf16[1,32,1,16,128]{4,3,2,1,0:T(8,128)(2,1)S(1)} %get-tuple-element.6), channel_id=1, source_target_pairs={{0,1},{1,2},{2,3},{4,5},{5,6},{6,7},{8,9},{9,10},{10,11},{12,13},{... | collective-permute-start | bytes 393224 | tf_op jit(solution)/shard_map/ppermute | solution.py:15
  13.2 1.3 collective-permute-start.1
  14.5 3.4 convert_reduce_fusion
  17.9 1.1 reshape_squeeze.3
  19.0 1.3 convolution_bitcast_fusion.1
  20.3 1.0 maximum_bitcast_fusion
  21.6 0.2 fusion.7
  21.8 0.2 fusion.9
  22.0 0.2 fusion.11
  22.2 0.2 fusion.13
  22.5 0.2 fusion.17
  22.7 0.2 fusion.19
  23.0 0.2 fusion.23
  23.2 0.2 fusion.25
  23.4 0.2 fusion.27
  23.6 0.2 fusion.29
  23.9 0.2 fusion.33
  24.1 0.2 fusion.35
  24.4 0.2 fusion.39
  24.6 0.2 fusion.41
  24.9 0.2 fusion.43
  25.1 0.2 fusion.45
  25.4 0.2 fusion.49
  25.6 4.6 %copy.25 = bf16[32,27,2,16,128]{4,3,2,1,0:T(8,128)(2,1)} copy(bf16[32,27,2,16,128]{4,3,2,0,1:T(8,128)(2,1)S(1)} %fusion.49) | data formatting | bytes 14155776 | tf_op jit(solution)/shard_map/stack | solution.py:44
  30.2 0.7 copy-done.1
  30.8 12.0 %subtract_convert_fusion = (bf16[32,27,2,16,128]{4,3,2,0,1:T(8,128)(2,1)}, bf16[32,27,2,16,128]{4,3,2,0,1:T(8,128)(2,1)}) fusion(bf16[32,27,2,16,128]{4,3,2,0,1:T(8,128)(2,1)} %copy-done.1, f32[2,16,128]{2,1,0:T(8,128)S(1)} %bitcast.151), kind=kLoop, calls=%fused_computation.2 | loop fusion | flops 21233664 | bytes 21250048 | tf_op jit(solution)/shard_map/convert_element_type | solution.py:56
  42.9 7.1 %copy.26 = bf16[32,27,2,16,128]{4,3,2,1,0:T(8,128)(2,1)} copy(bf16[32,27,2,16,128]{4,3,2,0,1:T(8,128)(2,1)} %get-tuple-element.5) | data formatting | bytes 14155776 | tf_op jit(solution)/shard_map/convert_element_type | solution.py:55
  50.0 11.6 %convert_element_type.83 = bf16[864,4096]{1,0:T(8,128)(2,1)} reshape(bf16[32,27,2,16,128]{4,3,2,1,0:T(8,128)(2,1)} %copy.26) | data formatting | bytes 14155776 | tf_op jit(solution)/shard_map/convert_element_type | solution.py:55
  61.6 11.6 %reshape.94 = bf16[864,4096]{1,0:T(8,128)(2,1)} reshape(bf16[32,27,2,16,128]{4,3,2,1,0:T(8,128)(2,1)} %copy.25) | data formatting | bytes 14155776 | tf_op jit(solution)/shard_map/reshape | solution.py:44
  73.2 7.1 %copy.27 = bf16[32,27,2,16,128]{4,3,2,1,0:T(8,128)(2,1)} copy(bf16[32,27,2,16,128]{4,3,2,0,1:T(8,128)(2,1)} %get-tuple-element.4) | data formatting | bytes 14155776 | tf_op jit(solution)/shard_map/convert_element_type | solution.py:56
  80.3 11.6 %convert_element_type.86 = bf16[864,4096]{1,0:T(8,128)(2,1)} reshape(bf16[32,27,2,16,128]{4,3,2,1,0:T(8,128)(2,1)} %copy.27) | data formatting | bytes 14155776 | tf_op jit(solution)/shard_map/convert_element_type | solution.py:56
  91.9 12.9 %fusion.60 = f32[864,864]{1,0:T(8,128)} fusion(bf16[864,4096]{1,0:T(8,128)(2,1)} %convert_element_type.83, bf16[864,4096]{1,0:T(8,128)(2,1)} %reshape.94), kind=kOutput, calls=%fused_computation.98 | convolution fusion | flops 6115295232 | bytes 17141760 | tf_op jit(solution)/shard_map/dot_general | solution.py:59
  104.8 5.1 %convolution_bitcast_fusion = f32[32,864]{1,0:T(8,128)S(1)} fusion(bf16[864,4096]{1,0:T(8,128)(2,1)} %reshape.94, bf16[32,4096]{1,0:T(8,128)(2,1)S(1)} %reshape_squeeze.3), kind=kOutput, calls=%fused_computation.32 | convolution fusion | flops 226492416 | bytes 7450624 | tf_op jit(solution)/shard_map/dot_general | solution.py:48
  109.9 0.7 pad_maximum_fusion
  110.7 13.3 %multiply_convert_fusion = bf16[864,864]{1,0:T(8,128)(2,1)} fusion(f32[864,864]{1,0:T(8,128)} %fusion.60, bf16[864,4096]{1,0:T(8,128)(2,1)} %convert_element_type.86, bf16[864,4096]{1,0:T(8,128)(2,1)} %reshape.94), kind=kOutput, calls=%fused_computation.30 | convolution fusion | flops 6117534720 | bytes 18634752 | tf_op jit(solution)/shard_map/dot_general | solution.py:60
  124.0 4.6 %reshape.96 = bf16[8,108,4,216]{3,2,1,0:T(4,128)(2,1)S(1)} reshape(bf16[864,864]{1,0:T(8,128)(2,1)} %multiply_convert_fusion) | data formatting | bytes 2985984 | tf_op jit(solution)/shard_map/reshape | solution.py:66
  128.6 2.6 copy.28
  131.2 4.4 %fusion.1 = bf16[4,8,32,128]{3,1,2,0:T(8,128)(2,1)S(1)} fusion(bf16[32,864]{1,0:T(8,128)(2,1)S(1)} %copy-done.2, bf16[864,4096]{1,0:T(8,128)(2,1)} %reshape.94), kind=kOutput, calls=%fused_computation.31 | convolution fusion | flops 226623488 | bytes 7395328 | tf_op jit(solution)/shard_map/dot_general | solution.py:46
  135.6 0.8 copy.32
  136.3 97.5 %all-reduce.5.cloned.1.call-done = f32[32,896]{1,0:T(8,128)} async-done(((f32[32,896]{1,0:T(8,128)}), f32[32,896]{1,0:T(8,128)}) %all-reduce.5.cloned.1.call-update) | async-done | bytes 114704 | tf_op jit(solution)/shard_map/psum | solution.py:72
  233.8 1.1 fusion.54
  235.0 1.3 fusion.56
  236.3 1.4 slice.130
  237.7 92.0 %reduce-scatter.4.cloned.1.call-done = bf16[1,108,216]{1,2,0:T(8,128)(2,1)} async-done(((bf16[32,108,216]{1,2,0:T(8,128)(2,1)}), bf16[1,108,216]{1,2,0:T(8,128)(2,1)}) %reduce-scatter.4.cloned.1.call-update) | async-done | bytes 46672
  329.7 1.5 bitcast_convert_fusion
  331.2 34.7 %all-reduce.7.cloned.1.call-done = f32[32,864]{1,0:T(8,128)} async-done(((f32[32,864]{1,0:T(8,128)}), f32[32,864]{1,0:T(8,128)}) %all-reduce.7.cloned.1.call-update) | async-done | bytes 110608 | tf_op jit(solution)/shard_map/psum | solution.py:78
  365.9 1.6 copy.63
  (25 shorter events, 1.1 us)
Async XLA Ops:
  7.2 227.8 %copy-start = (f32[216,864]{1,0:T(8,128)S(1)}, f32[216,864]{1,0:T(8,128)}, u32[]{:S(2)}) copy-start(f32[216,864]{1,0:T(8,128)} %param.10) | copy-start | bytes 2239492
  7.2 226.7 %all-reduce.5.cloned.1.call-start = ((), (), s32[]{:S(2)}) async-start(), calls=%async_computation.1 | async-start | bytes 229376 | tf_op jit(solution)/shard_map/psum | solution.py:72
  8.3 12.0 %collective-permute-start = (bf16[1,32,1,16,128]{4,3,2,1,0:T(8,128)(2,1)S(1)}, bf16[1,32,1,16,128]{4,3,2,1,0:T(8,128)(2,1)S(1)}, u32[]{:S(2)}, u32[]{:S(2)}) collective-permute-start(bf16[1,32,1,16,128]{4,3,2,1,0:T(8,128)(2,1)S(1)} %get-tuple-element.6), channel_id=1, source_target_pairs={{0,1},{1,2},{2,3},{4,5},{5,6},{6,7},{8,9},{9,10},{10,11},{12,13},{... | collective-permute-start | bytes 393224 | tf_op jit(solution)/shard_map/ppermute | solution.py:15
  13.2 7.0 %collective-permute-start.1 = (bf16[1,32,1,16,128]{4,3,2,1,0:T(8,128)(2,1)S(1)}, bf16[1,32,1,16,128]{4,3,2,1,0:T(8,128)(2,1)S(1)}, u32[]{:S(2)}, u32[]{:S(2)}) collective-permute-start(bf16[1,32,1,16,128]{4,3,2,1,0:T(8,128)(2,1)S(1)} %get-tuple-element.7), channel_id=1, source_target_pairs={{1,0},{2,1},{3,2},{5,4},{6,5},{7,6},{9,8},{10,9},{11,10},{13,12},{... | collective-permute-start | bytes 393224 | tf_op jit(solution)/shard_map/ppermute | solution.py:17
  25.6 5.3 %copy-start.1 = (bf16[32,27,2,16,128]{4,3,2,0,1:T(8,128)(2,1)}, bf16[32,27,2,16,128]{4,3,2,0,1:T(8,128)(2,1)S(1)}, u32[]{:S(2)}) copy-start(bf16[32,27,2,16,128]{4,3,2,0,1:T(8,128)(2,1)S(1)} %fusion.49) | copy-start | bytes 21233668
  110.7 219.0 %reduce-scatter.4.cloned.1.call-start = ((), (), s32[]{:S(2)}) async-start(), calls=%async_computation.3 | async-start | bytes 1824768
  124.0 7.2 %copy-start.2 = (bf16[32,864]{1,0:T(8,128)(2,1)S(1)}, bf16[32,864]{1,0:T(8,128)(2,1)}, u32[]{:S(2)}) copy-start(bf16[32,864]{1,0:T(8,128)(2,1)} %param.8) | copy-start | bytes 165892
  128.5 105.3 %copy-start.3 = (f32[32,32]{1,0:T(8,128)S(1)}, f32[32,32]{1,0:T(8,128)}, u32[]{:S(2)}) copy-start(f32[32,32]{1,0:T(8,128)} %param.11) | copy-start | bytes 12292
  131.1 234.7 %all-reduce.7.cloned.1.call-start = ((), (), s32[]{:S(2)}) async-start(), calls=%async_computation.2 | async-start | bytes 229376 | tf_op jit(solution)/shard_map/psum | solution.py:78
Sparse Core Ops, SparseCore 0:
  110.8 123.0 all-reduce.4
  239.2 90.4 reduce-scatter.3
  332.7 33.1 all-reduce.6
where the time goes:
time: 375 us; the launch traced here: 374 us
  waiting for transfers between devices  224 us (60%)
  local copies, waits for them, and re-layouts  71.4 us (19%)
  matrix products  39.4 us (11%)
  other arithmetic  18.6 us (5%)
  between operations  14 us (4%)
  starting transfers between devices  6.35 us (2%)
    psum x1, waiting for transfers between devices, on_device(): both = lax.psum(jnp.concatenate([grad_w, g_part], axis=1), ('dp', 'space'))  97.5 us
    unnamed x4, waiting for transfers between devices  92 us
    psum x1, waiting for transfers between devices, on_device(): lax.psum(jnp.dot(left_rows, a_inverse, precision=highest), 'space')  34.7 us
    convert_element_type x2, local copies, waits for them, and re-layouts, on_device(): high = weighted.astype(jnp.bfloat16)  18.8 us
    convert_element_type x2, local copies, waits for them, and re-layouts, on_device(): low = (weighted - high.astype(f32)).astype(jnp.bfloat16)  18.6 us
    dot_general x1, matrix products, on_device(): lax.dot_general(low, patches_t, contract_cells, preferred_element_type=f32)  13.3 us
    dot_general x1, matrix products, on_device(): lax.dot_general(high, patches_t, contract_cells, preferred_element_type=f32)  12.9 us
    convert_element_type x1, other arithmetic, on_device(): low = (weighted - high.astype(f32)).astype(jnp.bfloat16)  12 us
  transfers between devices with their start and end apart: 5, of which 3 were waited for; matrix products, arithmetic and copies ran while one was open for 10% of the time, Pallas kernels for 0%

commit v1 on v0

--- a/solution.py
+++ b/solution.py
@@ -69,7 +69,9 @@
     )
     a_factor = lax.psum_scatter(a_blocks, ("dp", "space"), scatter_dimension=0, tiled=True)
     a_factor = a_factor.reshape(rows, cols).astype(f32)
-    both = lax.psum(jnp.concatenate([grad_w, g_part], axis=1), ("dp", "space"))
+    both = jnp.sum(
+        lax.all_gather(jnp.concatenate([grad_w, g_part], axis=1), ("dp", "space")), axis=0
+    )
     grad_sum = both[:, :patch]
     g_factor = both[:, patch:]
     left = jnp.dot(g_inverse, grad_sum, precision=highest)

time: 375 us -> 267 us (0.71)
  waiting for transfers between devices: 224 us -> 118 us
  matrix products: 39.4 us -> 34.1 us
    psum x1 -> x0, waiting for transfers between devices: 97.5 us -> none  [on_device(): both = lax.psum(jnp.concatenate([grad_w, g_part], axis=1), ('dp', 'space'))]
    unnamed x4, waiting for transfers between devices: 92 us -> 81.3 us
    unnamed x36 -> x40, local copies, waits for them, and re-layouts: 6.94 us -> 9.2 us
  transfers between devices with their start and end apart: 5 -> 5, of which waited for: 3 -> 3; matrix products, arithmetic and copies ran while one was open for 10% -> 36% of each run, Pallas kernels for 0% -> 0%
where the time goes in v1:
time: 267 us; the launch traced here: 266 us
  waiting for transfers between devices  118 us (44%)
  local copies, waits for them, and re-layouts  72.4 us (27%)
  matrix products  34.1 us (13%)
  other arithmetic  20.3 us (8%)
  between operations  14 us (5%)
  starting transfers between devices  6.53 us (2%)
    unnamed x4, waiting for transfers between devices  81.3 us
    psum x1, waiting for transfers between devices, on_device(): lax.psum(jnp.dot(left_rows, a_inverse, precision=highest), 'space')  34 us
    convert_element_type x2, local copies, waits for them, and re-layouts, on_device(): low = (weighted - high.astype(f32)).astype(jnp.bfloat16)  18.8 us
    convert_element_type x2, local copies, waits for them, and re-layouts, on_device(): high = weighted.astype(jnp.bfloat16)  18.7 us
    convert_element_type x1, other arithmetic, on_device(): low = (weighted - high.astype(f32)).astype(jnp.bfloat16)  12 us
    reshape x1, local copies, waits for them, and re-layouts, on_device(): patches_t = jnp.stack(taps, axis=1).reshape(patch, cells)  11.6 us
    dot_general x1, matrix products, on_device(): lax.dot_general(high, patches_t, contract_cells, preferred_element_type=f32)  11 us
    dot_general x1, matrix products, on_device(): lax.dot_general(low, patches_t, contract_cells, preferred_element_type=f32)  10.8 us
  transfers between devices with their start and end apart: 5, of which 3 were waited for; matrix products, arithmetic and copies ran while one was open for 36% of the time, Pallas kernels for 0%

profile of v1, /device:TPU:0, one launch (start us, length us, event | category | flops | bytes accessed | tf_op | source)
XLA Modules:
  0.0 265.8 jit_solution(1556473297271966058)
XLA Ops:
  7.2 1.1 fusion.59
  8.3 4.9 %collective-permute-start = (bf16[1,32,1,16,128]{4,3,2,1,0:T(8,128)(2,1)S(1)}, bf16[1,32,1,16,128]{4,3,2,1,0:T(8,128)(2,1)S(1)}, u32[]{:S(2)}, u32[]{:S(2)}) collective-permute-start(bf16[1,32,1,16,128]{4,3,2,1,0:T(8,128)(2,1)S(1)} %get-tuple-element.6), channel_id=1, source_target_pairs={{0,1},{1,2},{2,3},{4,5},{5,6},{6,7},{8,9},{9,10},{10,11},{12,13},{... | collective-permute-start | bytes 393224 | tf_op jit(solution)/shard_map/ppermute | solution.py:15
  13.2 1.3 collective-permute-start.1
  14.5 1.1 reshape_squeeze.3
  15.6 1.3 convolution_bitcast_fusion.1
  16.9 3.2 %collective-permute-done.1 = bf16[1,32,1,16,128]{4,3,2,1,0:T(8,128)(2,1)S(1)} collective-permute-done((bf16[1,32,1,16,128]{4,3,2,1,0:T(8,128)(2,1)S(1)}, bf16[1,32,1,16,128]{4,3,2,1,0:T(8,128)(2,1)S(1)}, u32[]{:S(2)}, u32[]{:S(2)}) %collective-permute-start.1) | collective-permute-done | bytes 131104 | tf_op jit(solution)/shard_map/ppermute | solution.py:17
  20.1 1.0 maximum_bitcast_fusion
  21.4 0.2 fusion.7
  21.6 0.2 fusion.9
  21.8 0.2 fusion.11
  22.0 0.2 fusion.13
  22.3 0.2 fusion.17
  22.5 0.2 fusion.19
  22.8 0.2 fusion.23
  23.0 0.2 fusion.25
  23.4 0.2 fusion.29
  23.7 0.2 fusion.33
  23.9 0.2 fusion.35
  24.2 0.2 fusion.39
  24.4 0.2 fusion.41
  24.9 0.2 fusion.45
  25.2 0.2 fusion.49
  25.4 2.9 %copy-done.1 = bf16[32,27,2,16,128]{4,3,2,0,1:T(8,128)(2,1)} copy-done((bf16[32,27,2,16,128]{4,3,2,0,1:T(8,128)(2,1)}, bf16[32,27,2,16,128]{4,3,2,0,1:T(8,128)(2,1)S(1)}, u32[]{:S(2)}) %copy-start.1) | copy-done | bytes 7077912
  28.3 4.0 %copy.25 = bf16[32,27,2,16,128]{4,3,2,1,0:T(8,128)(2,1)} copy(bf16[32,27,2,16,128]{4,3,2,0,1:T(8,128)(2,1)S(1)} %fusion.49) | data formatting | bytes 14155776 | tf_op jit(solution)/shard_map/stack | solution.py:44
  32.3 11.6 %reshape.94 = bf16[864,4096]{1,0:T(8,128)(2,1)} reshape(bf16[32,27,2,16,128]{4,3,2,1,0:T(8,128)(2,1)} %copy.25) | data formatting | bytes 14155776 | tf_op jit(solution)/shard_map/reshape | solution.py:44
  43.9 5.1 %convolution_bitcast_fusion = f32[32,864]{1,0:T(8,128)S(1)} fusion(bf16[864,4096]{1,0:T(8,128)(2,1)} %reshape.94, bf16[32,4096]{1,0:T(8,128)(2,1)S(1)} %reshape_squeeze.3), kind=kOutput, calls=%fused_computation.32 | convolution fusion | flops 226492416 | bytes 7450624 | tf_op jit(solution)/shard_map/dot_general | solution.py:48
  49.1 0.7 pad_maximum_fusion
  49.8 0.2 reduce-scatter.4.cloned.1.call-start
  50.1 2.8 %convert_reduce_fusion = f32[4096]{0:T(1024)S(1)} fusion(s32[1024]{0:T(1024)S(1)} %bitcast.154), kind=kLoop, calls=%fused_computation | loop fusion | flops 12578816 | bytes 20480 | tf_op jit(solution)/shard_map/reduce_sum | solution.py:51
  52.8 12.0 %subtract_convert_fusion = (bf16[32,27,2,16,128]{4,3,2,0,1:T(8,128)(2,1)}, bf16[32,27,2,16,128]{4,3,2,0,1:T(8,128)(2,1)}) fusion(bf16[32,27,2,16,128]{4,3,2,0,1:T(8,128)(2,1)} %copy-done.1, f32[2,16,128]{2,1,0:T(8,128)S(1)} %bitcast.153), kind=kLoop, calls=%fused_computation.2 | loop fusion | flops 21233664 | bytes 21250048 | tf_op jit(solution)/shard_map/convert_element_type | solution.py:56
  64.9 7.1 %copy.26 = bf16[32,27,2,16,128]{4,3,2,1,0:T(8,128)(2,1)} copy(bf16[32,27,2,16,128]{4,3,2,0,1:T(8,128)(2,1)} %get-tuple-element.5) | data formatting | bytes 14155776 | tf_op jit(solution)/shard_map/convert_element_type | solution.py:55
  71.9 11.6 %convert_element_type.83 = bf16[864,4096]{1,0:T(8,128)(2,1)} reshape(bf16[32,27,2,16,128]{4,3,2,1,0:T(8,128)(2,1)} %copy.26) | data formatting | bytes 14155776 | tf_op jit(solution)/shard_map/convert_element_type | solution.py:55
  83.5 7.2 %copy.27 = bf16[32,27,2,16,128]{4,3,2,1,0:T(8,128)(2,1)} copy(bf16[32,27,2,16,128]{4,3,2,0,1:T(8,128)(2,1)} %get-tuple-element.4) | data formatting | bytes 14155776 | tf_op jit(solution)/shard_map/convert_element_type | solution.py:56
  90.7 11.6 %convert_element_type.86 = bf16[864,4096]{1,0:T(8,128)(2,1)} reshape(bf16[32,27,2,16,128]{4,3,2,1,0:T(8,128)(2,1)} %copy.27) | data formatting | bytes 14155776 | tf_op jit(solution)/shard_map/convert_element_type | solution.py:56
  102.3 11.0 %fusion.60 = f32[864,864]{1,0:T(8,128)S(1)} fusion(bf16[864,4096]{1,0:T(8,128)(2,1)} %convert_element_type.83, bf16[864,4096]{1,0:T(8,128)(2,1)} %reshape.94), kind=kOutput, calls=%fused_computation.98 | convolution fusion | flops 6115295232 | bytes 17141760 | tf_op jit(solution)/shard_map/dot_general | solution.py:59
  113.4 10.8 %multiply_convert_fusion = bf16[864,864]{1,0:T(8,128)(2,1)} fusion(f32[864,864]{1,0:T(8,128)S(1)} %fusion.60, bf16[864,4096]{1,0:T(8,128)(2,1)S(1)} %copy-done.2, bf16[864,4096]{1,0:T(8,128)(2,1)} %reshape.94), kind=kOutput, calls=%fused_computation.30 | convolution fusion | flops 6117534720 | bytes 18634752 | tf_op jit(solution)/shard_map/dot_general | solution.py:60
  124.2 4.6 %reshape.96 = bf16[8,108,4,216]{3,2,1,0:T(4,128)(2,1)S(1)} reshape(bf16[864,864]{1,0:T(8,128)(2,1)} %multiply_convert_fusion) | data formatting | bytes 2985984 | tf_op jit(solution)/shard_map/reshape | solution.py:66
  128.8 2.5 copy.28
  131.4 4.3 %fusion.1 = bf16[4,8,32,128]{3,1,2,0:T(8,128)(2,1)S(1)} fusion(bf16[32,864]{1,0:T(8,128)(2,1)S(1)} %copy-done.3, bf16[864,4096]{1,0:T(8,128)(2,1)} %reshape.94), kind=kOutput, calls=%fused_computation.31 | convolution fusion | flops 226623488 | bytes 7395328 | tf_op jit(solution)/shard_map/dot_general | solution.py:46
  135.7 0.8 copy.32
  136.5 2.2 reduce_sum.19
  138.8 0.2 fusion.54
  139.0 1.3 fusion.56
  140.3 81.2 %reduce-scatter.4.cloned.1.call-done = bf16[1,108,216]{1,2,0:T(8,128)(2,1)} async-done(((bf16[32,108,216]{1,2,0:T(8,128)(2,1)}), bf16[1,108,216]{1,2,0:T(8,128)(2,1)}) %reduce-scatter.4.cloned.1.call-update) | async-done | bytes 46672
  221.5 1.5 bitcast_convert_fusion
  223.0 0.7 slice.130
  223.7 34.0 %all-reduce.4.cloned.1.call-done = f32[32,864]{1,0:T(8,128)} async-done(((f32[32,864]{1,0:T(8,128)}), f32[32,864]{1,0:T(8,128)}) %all-reduce.4.cloned.1.call-update) | async-done | bytes 110608 | tf_op jit(solution)/shard_map/psum | solution.py:80
  257.7 1.6 copy.62
  (30 shorter events, 1.4 us)
Async XLA Ops:
  7.2 131.8 %copy-start = (f32[216,864]{1,0:T(8,128)S(1)}, f32[216,864]{1,0:T(8,128)}, u32[]{:S(2)}) copy-start(f32[216,864]{1,0:T(8,128)} %param.10) | copy-start | bytes 2239492
  7.2 129.3 %all-gather.3.cloned.1.call-start = ((), (), s32[]{:S(2)}) async-start(), calls=%async_computation.2 | async-start | bytes 3784704 | tf_op jit(solution)/shard_map/all_gather | solution.py:73
  8.3 8.6 %collective-permute-start = (bf16[1,32,1,16,128]{4,3,2,1,0:T(8,128)(2,1)S(1)}, bf16[1,32,1,16,128]{4,3,2,1,0:T(8,128)(2,1)S(1)}, u32[]{:S(2)}, u32[]{:S(2)}) collective-permute-start(bf16[1,32,1,16,128]{4,3,2,1,0:T(8,128)(2,1)S(1)} %get-tuple-element.6), channel_id=1, source_target_pairs={{0,1},{1,2},{2,3},{4,5},{5,6},{6,7},{8,9},{9,10},{10,11},{12,13},{... | collective-permute-start | bytes 393224 | tf_op jit(solution)/shard_map/ppermute | solution.py:15
  13.2 6.9 %collective-permute-start.1 = (bf16[1,32,1,16,128]{4,3,2,1,0:T(8,128)(2,1)S(1)}, bf16[1,32,1,16,128]{4,3,2,1,0:T(8,128)(2,1)S(1)}, u32[]{:S(2)}, u32[]{:S(2)}) collective-permute-start(bf16[1,32,1,16,128]{4,3,2,1,0:T(8,128)(2,1)S(1)} %get-tuple-element.7), channel_id=1, source_target_pairs={{1,0},{2,1},{3,2},{5,4},{6,5},{7,6},{9,8},{10,9},{11,10},{13,12},{... | collective-permute-start | bytes 393224 | tf_op jit(solution)/shard_map/ppermute | solution.py:17
  25.4 2.9 %copy-start.1 = (bf16[32,27,2,16,128]{4,3,2,0,1:T(8,128)(2,1)}, bf16[32,27,2,16,128]{4,3,2,0,1:T(8,128)(2,1)S(1)}, u32[]{:S(2)}) copy-start(bf16[32,27,2,16,128]{4,3,2,0,1:T(8,128)(2,1)S(1)} %fusion.49) | copy-start | bytes 21233668
  43.9 6.1 %copy-start.5 = (s32[1,1024]{1,0:T(1,128)S(1)}, s32[1,1024]{1,0:T(1,128)}, u32[]{:S(2)}) copy-start(s32[1,1024]{1,0:T(1,128)} %param.9) | copy-start | bytes 12292
  49.8 171.7 %reduce-scatter.4.cloned.1.call-start = ((), (), s32[]{:S(2)}) async-start(), calls=%async_computation.3 | async-start | bytes 1824768
  102.3 11.0 %copy-start.2 = (bf16[864,4096]{1,0:T(8,128)(2,1)S(1)}, bf16[864,4096]{1,0:T(8,128)(2,1)}, u32[]{:S(2)}) copy-start(bf16[864,4096]{1,0:T(8,128)(2,1)} %convert_element_type.86) | copy-start | bytes 21233668
  124.2 7.2 %copy-start.3 = (bf16[32,864]{1,0:T(8,128)(2,1)S(1)}, bf16[32,864]{1,0:T(8,128)(2,1)}, u32[]{:S(2)}) copy-start(bf16[32,864]{1,0:T(8,128)(2,1)} %param.8) | copy-start | bytes 165892
  131.3 7.4 %copy-start.4 = (f32[32,32]{1,0:T(8,128)S(1)}, f32[32,32]{1,0:T(8,128)}, u32[]{:S(2)}) copy-start(f32[32,32]{1,0:T(8,128)} %param.11) | copy-start | bytes 12292
  131.3 126.4 %all-reduce.4.cloned.1.call-start = ((), (), s32[]{:S(2)}) async-start(), calls=%async_computation.1 | async-start | bytes 229376 | tf_op jit(solution)/shard_map/psum | solution.py:80
Sparse Core Ops, SparseCore 0:
  49.9 60.6 all-gather.2
  131.5 90.0 reduce-scatter.3
  224.5 33.1 all-reduce.3
